TPU v7x, 512 devices: a whole 4x4x16 slice. The times are simulated.
512 devices in a mesh: row: 64 (over z, x), rep: 8 (over y, core).
Axes of the slice: x: 4, y: 4, z: 16, core: 2. Of those that a mesh axis runs over, the one named last changes fastest.
Arguments:
- features: bfloat16 [16384, 128], P('row', 'rep'), may hold values from -6 to 6
- owner_index: int32 [16384], P('row'), may hold values from 0 to 16383, as said below
- block_cols: int32 [128, 64], P('row', 'rep'), may hold values from 0 to 127, as said below
- block_count: int32 [128], P('row'), may hold values from 1 to 64, as said below
- tiles: bfloat16 [128, 64, 128, 128], P('row', 'rep'), may hold values from -0.109375 to 0.109375
- weight: bfloat16 [128, 256], P(None, 'rep'), may hold values from -0.75 to 0.75
- bias: float32 [256], P('rep'), may hold values from -4 to 4
- grad_out: bfloat16 [16384, 256], P('row', 'rep'), may hold values from -6 to 6
Outputs:
- hidden: bfloat16 [16384, 256], P('row', 'rep')
- weight_grad: float32 [128, 256], P(None, 'rep')
- bias_grad: float32 [256], P('rep')
Inputs may be any that keep to these rules, and one draw needn't show every extreme that they name: `owner_index`: A permutation; the 256 rows of each loader shard hold exactly 4 positions of every partition's 2*128 rows. `block_cols`: the block columns of one block row are distinct. Block column c belongs to partition c // 2. Over all slots of one partition's 2 block rows, exactly 1 distinct block columns of each partition are named. `block_count`: some block row has all 64 slots live.
All inputs are finite; a program needn't handle non-finite values.
Results may differ from a plain program's by a relative error of at most 0.017.
Values may be sent and summed in bfloat16 or wider, within the bound.
No kernel may reach another device: no remote copies, remote signals or barrier semaphores. Data moves between devices by JAX's collectives and lax.ppermute only.
A program may use at most 64 MiB of HBM per device.

v0:
```python
import jax
import jax.numpy as jnp
from jax import lax
from jax.sharding import PartitionSpec as P


def sum_over(x, axis_name, count):
    rows = x.shape[0]
    pieces = x.reshape((count, rows // count) + x.shape[1:])
    got = lax.all_to_all(pieces, axis_name, 0, 0, tiled=True)
    reduced = jnp.sum(got.astype(jnp.float32), axis=0)
    return reduced


def spread(x, axis_name, count):
    wide = jnp.broadcast_to(x[None], (count,) + x.shape)
    return lax.all_to_all(wide, axis_name, 0, 0, tiled=True)


def on_device(features, owner_index, block_cols, block_count, tiles, weight, bias, grad_out):
    rows_part, cols_dev = features.shape
    parts = lax.axis_size("row")
    reps = lax.axis_size("rep")
    per_pair = rows_part // parts
    rb, slots_dev, size_blk = (tiles.shape[0], tiles.shape[1], tiles.shape[2])
    destination = owner_index // rows_part
    same = destination[:, None] == destination[None, :]
    before = jnp.arange(rows_part)[:, None] > jnp.arange(rows_part)[None, :]
    rank = jnp.sum(same & before, axis=1)
    slot = rank * parts + destination
    place = (slot[:, None] == jnp.arange(rows_part)[None, :]).astype(jnp.bfloat16)
    pos_row = (owner_index % rows_part).astype(jnp.bfloat16)
    loader = jnp.concatenate([features.T, pos_row[None, :]], axis=0)
    packet = jnp.dot(loader, place, preferred_element_type=jnp.float32).astype(jnp.bfloat16)
    width = cols_dev + 1
    packet = packet.reshape(width, per_pair, parts)
    wide = jnp.broadcast_to(packet[None], (parts,) + packet.shape)
    grouped = lax.all_to_all(wide, "row", 0, 2, tiled=True)[0]
    pos = grouped[cols_dev].T.astype(jnp.int32)
    values = grouped[:cols_dev]
    cols_all = lax.all_gather(block_cols, "rep", axis=1, tiled=True)
    part_of = cols_all // rb
    half_of = cols_all % rb
    part_ids = jnp.arange(parts, dtype=jnp.int32)
    hit = part_of[None, :, :] == part_ids[:, None, None]
    half = jnp.max(jnp.where(hit, half_of[None, :, :], 0), axis=(1, 2))
    node_ids = jnp.arange(size_blk, dtype=jnp.int32)
    target = half[:, None, None] * size_blk + node_ids[None, None, :]
    pick = (pos[:, :, None] == target).astype(jnp.bfloat16)
    needed = jnp.einsum("fgq,qgn->qfn", grouped, pick, preferred_element_type=jnp.float32).astype(
        jnp.bfloat16
    )
    needed = needed[:, :cols_dev, :]
    peer_parts = part_of.reshape(rb, reps, slots_dev).transpose(1, 0, 2).reshape(-1)
    choose = (peer_parts[:, None] == part_ids[None, :]).astype(jnp.bfloat16)
    outgoing = jnp.dot(choose, needed.reshape(parts, -1), preferred_element_type=jnp.float32)
    outgoing = outgoing.astype(jnp.bfloat16).reshape(reps, rb, slots_dev, cols_dev, size_blk)
    incoming = lax.all_to_all(outgoing, "rep", 0, 0, tiled=True)
    slot_ids = lax.axis_index("rep") * slots_dev + jnp.arange(slots_dev, dtype=jnp.int32)
    live = slot_ids[None, :] < block_count[:, None]
    tiles_live = jnp.where(live[:, :, None, None], tiles, jnp.zeros_like(tiles))
    partial = jnp.einsum(
        "rsin,jrsfn->rijf", tiles_live, incoming, preferred_element_type=jnp.float32
    )
    partial = partial.reshape(rows_part, reps * cols_dev)
    shares = spread(partial.astype(jnp.bfloat16), "rep", reps)
    agg = jnp.sum(shares.astype(jnp.float32), axis=0).astype(jnp.bfloat16)
    pre = jnp.dot(agg, weight, preferred_element_type=jnp.float32) + bias
    hidden = jax.nn.silu(pre).astype(jnp.bfloat16)
    sig = jax.nn.sigmoid(pre)
    dpre = (grad_out.astype(jnp.float32) * sig * (1.0 + pre * (1.0 - sig))).astype(jnp.bfloat16)
    weight_term = jnp.dot(agg.T, dpre, preferred_element_type=jnp.float32)
    bias_term = jnp.sum(dpre.astype(jnp.float32), axis=0)
    n_in, n_out = weight_term.shape
    bias_row = jnp.pad(bias_term, (0, n_in - n_out))[None, :]
    stacked = jnp.concatenate([weight_term.T, bias_row], axis=0)
    per = -(-stacked.shape[0] // parts)
    stacked = jnp.pad(stacked, ((0, parts * per - stacked.shape[0]), (0, 0)))
    total = spread(sum_over(stacked, "row", parts), "row", parts).reshape(parts * per, n_in)
    weight_grad = total[:n_out].T
    bias_grad = total[n_out, :n_out]
    return (hidden, weight_grad, bias_grad)


def solution(mesh):
    placed = (
        P("row", "rep"),
        P("row"),
        P("row", "rep"),
        P("row"),
        P("row", "rep", None, None),
        P(None, "rep"),
        P("rep"),
        P("row", "rep"),
    )
    return jax.shard_map(
        on_device,
        mesh=mesh,
        in_specs=placed,
        out_specs=(P("row", "rep"), P(None, "rep"), P("rep")),
        check_vma=False,
    )
```

profile of v0, /device:TPU:8, one launch (start us, length us, event | category | flops | bytes accessed | tf_op | source)
XLA Modules:
  0.0 133.0 jit_solution(4461811390317609364)
XLA Ops:
  0.6 0.0 copy-start
  0.6 0.7 fusion.18
  1.3 0.2 convert_reduce_fusion
  1.5 0.9 convolution_convert_fusion.1
  2.5 0.1 broadcast_in_dim.37
  2.6 0.3 broadcast_in_dim.38
  2.9 0.0 copy-start.1
  2.9 1.6 %reshape.116 = bf16[64,2,2176]{2,1,0:T(2,128)(2,1)} reshape(bf16[64,17,4,64]{3,2,1,0:T(4,128)(2,1)S(1)} %broadcast_in_dim.38) | data formatting | bytes 1114112
  4.5 18.6 %all-to-all-start = ((bf16[64,2,2176]{2,1,0:T(2,128)(2,1)}), bf16[64,2,2176]{2,1,0:T(2,128)(2,1)S(1)}, u32[]{:S(2)}, u32[]{:S(2)}) async-start(bf16[64,2,2176]{2,1,0:T(2,128)(2,1)} %reshape.116), calls=%async_computation | async-start | bytes 1114112 | tf_op jit(solution)/shard_map/all_to_all | solution.py:38
  23.0 0.0 copy-done.1
  23.0 8.8 %all-gather = s32[8,8,2]{1,2,0:T(2,128)S(1)} all-gather(s32[1,8,2]{1,2,0:T(2,128)S(1)} %bitcast.85), channel_id=1, replica_groups=mesh['row'=64,'rep'=8] {'rep'}, dimensions={0}, use_global_device_ids=true | all-gather | bytes 576 | tf_op jit(solution)/shard_map/all_gather | solution.py:41
  31.8 0.1 reshape.113
  31.9 0.1 reshape.106
  32.0 0.1 eq.34
  32.1 0.1 select_reduce_fusion
  32.2 0.1 iota_add_fusion
  32.3 25.0 %all-to-all-done = bf16[64,2,2176]{2,1,0:T(2,128)(2,1)S(1)} async-done(((bf16[64,2,2176]{2,1,0:T(2,128)(2,1)}), bf16[64,2,2176]{2,1,0:T(2,128)(2,1)S(1)}, u32[]{:S(2)}, u32[]{:S(2)}) %all-to-all-start) | async-done | bytes 557088 | tf_op jit(solution)/shard_map/all_to_all | solution.py:38
  57.3 0.7 reshape.117
  58.0 0.5 copy.34
  58.5 0.8 copy.36
  59.4 0.1 copy.35
  59.5 3.7 %fusion = bf16[64,17,128]{2,1,0:T(8,128)(2,1)S(1)} fusion(bf16[17,256,64]{1,0,2:T(8,128)(2,1)S(1)} %copy.36, s32[64,128]{1,0:T(8,128)S(1)} %iota_add_fusion, s32[64,256]{1,0:T(8,128)S(1)} %copy.35), kind=kOutput, calls=%fused_computation | convolution fusion | flops 73400320 | bytes 933888 | tf_op jit(solution)/shard_map/fgq,qgn->qfn/dot_general | solution.py:50
  63.3 0.3 convolution_convert_fusion
  63.6 0.0 copy-start.4
  63.6 0.0 copy-start.2
  63.6 0.9 copy.37
  64.5 4.9 %all-to-all-start.1 = ((bf16[8,2,8,16,128]{4,3,2,1,0:T(8,128)(2,1)}), bf16[8,2,8,16,128]{4,3,2,1,0:T(8,128)(2,1)S(1)}, u32[]{:S(2)}, u32[]{:S(2)}) async-start(bf16[8,2,8,16,128]{4,3,2,1,0:T(8,128)(2,1)} %copy.37), calls=%async_computation.1 | async-start | bytes 1048576 | tf_op jit(solution)/shard_map/all_to_all | solution.py:58
  69.5 0.0 copy-done.4
  69.5 0.1 broadcast_compare_fusion.3
  69.5 8.8 %all-to-all-done.1 = bf16[8,2,8,16,128]{4,3,2,1,0:T(8,128)(2,1)S(1)} async-done(((bf16[8,2,8,16,128]{4,3,2,1,0:T(8,128)(2,1)}), bf16[8,2,8,16,128]{4,3,2,1,0:T(8,128)(2,1)S(1)}, u32[]{:S(2)}, u32[]{:S(2)}) %all-to-all-start.1) | async-done | bytes 524320 | tf_op jit(solution)/shard_map/all_to_all | solution.py:58
  78.3 0.0 copy-done.2
  78.3 0.4 fusion.4
  78.7 0.1 copy.39
  78.8 0.1 copy.40
  78.9 0.0 copy-start.3
  78.9 0.0 copy-start.5
  79.0 0.1 broadcast_in_dim.41
  79.0 12.8 %all_to_all.35 = bf16[8,256,128]{2,1,0:T(8,128)(2,1)S(1)} all-to-all(bf16[8,256,128]{2,1,0:T(8,128)(2,1)S(1)} %broadcast_in_dim.41), channel_id=1, replica_groups=mesh['row'=64,'rep'=8] {'rep'}, dimensions={0} | all-to-all | bytes 1048576 | tf_op jit(solution)/shard_map/all_to_all | solution.py:17
  91.8 0.1 reduce_sum.40
  91.9 0.0 copy-done
  91.9 0.0 copy-done.3
  92.0 0.9 convert_reduce_fusion.1
  92.8 0.1 fusion.21
  93.0 20.2 %all_to_all.36 = f32[64,1,128]{2,1,0:T(1,128)S(1)} all-to-all(f32[64,1,128]{2,1,0:T(1,128)S(1)} %bitcast.81), channel_id=1, replica_groups=mesh['row'=64,'rep'=8] {'row'}, dimensions={0} | all-to-all | bytes 65536 | tf_op jit(solution)/shard_map/all_to_all | solution.py:10
  113.2 0.1 reduce_sum.42
  113.3 18.5 %all_to_all.37 = f32[64,1,128]{2,1,0:T(1,128)S(1)} all-to-all(f32[64,1,128]{2,1,0:T(1,128)S(1)} %broadcast_in_dim.43), channel_id=1, replica_groups=mesh['row'=64,'rep'=8] {'row'}, dimensions={0} | all-to-all | bytes 65536 | tf_op jit(solution)/shard_map/all_to_all | solution.py:17
  131.8 0.5 slice_bitcast_fusion
  132.4 0.6 slice.23
  (15 shorter events, 0.2 us)
Async XLA Ops:
  0.6 91.3 %copy-start = (bf16[128,32]{0,1:T(8,128)(2,1)S(1)}, bf16[128,32]{0,1:T(8,128)(2,1)}, u32[]{:S(2)}) copy-start(bf16[128,32]{0,1:T(8,128)(2,1)} %param.13) | copy-start | bytes 24580
  2.9 20.2 %copy-start.1 = (s32[2,8]{1,0:T(2,128)S(1)}, s32[2,8]{1,0:T(2,128)}, u32[]{:S(2)}) copy-start(s32[2,8]{1,0:T(2,128)} %param.10) | copy-start | bytes 196
  4.5 52.8 %all-to-all-start = ((bf16[64,2,2176]{2,1,0:T(2,128)(2,1)}), bf16[64,2,2176]{2,1,0:T(2,128)(2,1)S(1)}, u32[]{:S(2)}, u32[]{:S(2)}) async-start(bf16[64,2,2176]{2,1,0:T(2,128)(2,1)} %reshape.116), calls=%async_computation | async-start | bytes 1114112 | tf_op jit(solution)/shard_map/all_to_all | solution.py:38
  63.6 5.8 %copy-start.4 = (s32[2]{0:T(128)S(1)}, s32[2]{0:T(128)}, u32[]{:S(2)}) copy-start(s32[2]{0:T(128)} %param.11) | copy-start | bytes 28
  63.6 14.7 %copy-start.2 = (bf16[2,8,128,128]{3,2,1,0:T(8,128)(2,1)S(1)}, bf16[2,8,128,128]{3,2,1,0:T(8,128)(2,1)}, u32[]{:S(2)}) copy-start(bf16[2,8,128,128]{3,2,1,0:T(8,128)(2,1)} %param.12) | copy-start | bytes 1572868
  64.5 13.8 %all-to-all-start.1 = ((bf16[8,2,8,16,128]{4,3,2,1,0:T(8,128)(2,1)}), bf16[8,2,8,16,128]{4,3,2,1,0:T(8,128)(2,1)S(1)}, u32[]{:S(2)}, u32[]{:S(2)}) async-start(bf16[8,2,8,16,128]{4,3,2,1,0:T(8,128)(2,1)} %copy.37), calls=%async_computation.1 | async-start | bytes 1048576 | tf_op jit(solution)/shard_map/all_to_all | solution.py:58
  78.9 13.0 %copy-start.3 = (bf16[256,32]{0,1:T(8,128)(2,1)S(1)}, bf16[256,32]{0,1:T(8,128)(2,1)}, u32[]{:S(2)}) copy-start(bf16[256,32]{0,1:T(8,128)(2,1)} %param.15) | copy-start | bytes 49156
  78.9 13.0 %copy-start.5 = (f32[32]{0:T(128)S(1)}, f32[32]{0:T(128)}, u32[]{:S(2)}) copy-start(f32[32]{0:T(128)} %param.14) | copy-start | bytes 388
where the time goes:
time: 133 us
  blocking collectives  60.3 us (45%)
  waiting for transfers between devices  33.8 us (25%)
  starting transfers between devices  23.5 us (18%)
  local copies, waits for them, and re-layouts  6.78 us (5%)
  matrix products  6.39 us (5%)
  other arithmetic  1.35 us (1%)
    all_to_all x2, blocking collectives, spread(): return lax.all_to_all(wide, axis_name, 0, 0, tiled=True)  31.3 us
    all_to_all x1, waiting for transfers between devices, on_device(): grouped = lax.all_to_all(wide, 'row', 0, 2, tiled=True)[0]  25 us
    all_to_all x1, blocking collectives, sum_over(): got = lax.all_to_all(pieces, axis_name, 0, 0, tiled=True)  20.2 us
    all_to_all x1, starting transfers between devices, on_device(): grouped = lax.all_to_all(wide, 'row', 0, 2, tiled=True)[0]  18.6 us
    all_to_all x1, waiting for transfers between devices, on_device(): incoming = lax.all_to_all(outgoing, 'rep', 0, 0, tiled=True)  8.81 us
    all_gather x1, blocking collectives, on_device(): cols_all = lax.all_gather(block_cols, 'rep', axis=1, tiled=True)  8.77 us
    all_to_all x1, starting transfers between devices, on_device(): incoming = lax.all_to_all(outgoing, 'rep', 0, 0, tiled=True)  4.92 us
    dot_general x1, matrix products, on_device(): jnp.einsum('fgq,qgn->qfn', grouped, pick, preferred_element_type=jnp.floa...  3.74 us
  transfers between devices with their start and end apart: 2, of which 2 were waited for; matrix products, arithmetic and copies ran while one was open for 0% of the time, Pallas kernels for 0%

commit v1 on v0

--- a/solution.py
+++ b/solution.py
@@ -38,7 +38,8 @@
     grouped = lax.all_to_all(wide, "row", 0, 2, tiled=True)[0]
     pos = grouped[cols_dev].T.astype(jnp.int32)
     values = grouped[:cols_dev]
-    cols_all = lax.all_gather(block_cols, "rep", axis=1, tiled=True)
+    sent = jnp.stack([block_cols] * lax.axis_size("rep"))
+    cols_all = jnp.concatenate(lax.all_to_all(sent, "rep", 0, 0), axis=1)
     part_of = cols_all // rb
     half_of = cols_all % rb
     part_ids = jnp.arange(parts, dtype=jnp.int32)

time: 133 us -> 140 us (1.053)
  waiting for transfers between devices: 33.8 us -> 42.9 us
  blocking collectives: 60.3 us -> 51.6 us
  starting transfers between devices: 23.5 us -> 28.3 us
    all_to_all x1, waiting for transfers between devices: 25 us -> 34.1 us  [on_device(): grouped = lax.all_to_all(wide, 'row', 0, 2, tiled=True)[0]]
    all_to_all x0 -> x1, starting transfers between devices: none -> 9.07 us  [on_device(): cols_all = jnp.concatenate(lax.all_to_all(sent, 'rep', 0, 0), axis=1)]
    all_gather x1 -> x0, blocking collectives: 8.77 us -> none  [on_device(): cols_all = lax.all_gather(block_cols, 'rep', axis=1, tiled=True)]
    all_to_all x1, starting transfers between devices: 18.6 us -> 14.4 us  [on_device(): grouped = lax.all_to_all(wide, 'row', 0, 2, tiled=True)[0]]
  transfers between devices with their start and end apart: 2 -> 3, of which waited for: 2 -> 3; matrix products, arithmetic and copies ran while one was open for 0% -> 3% of each run, Pallas kernels for 0% -> 0%
where the time goes in v1:
time: 140 us; the launch traced here: 139 us
  blocking collectives  51.6 us (37%)
  waiting for transfers between devices  42.9 us (31%)
  starting transfers between devices  28.3 us (20%)
  local copies, waits for them, and re-layouts  7.96 us (6%)
  matrix products  6.39 us (5%)
    all_to_all x1, waiting for transfers between devices, on_device(): grouped = lax.all_to_all(wide, 'row', 0, 2, tiled=True)[0]  34.1 us
    all_to_all x2, blocking collectives, spread(): return lax.all_to_all(wide, axis_name, 0, 0, tiled=True)  31.3 us
    all_to_all x1, blocking collectives, sum_over(): got = lax.all_to_all(pieces, axis_name, 0, 0, tiled=True)  20.2 us
    all_to_all x1, starting transfers between devices, on_device(): grouped = lax.all_to_all(wide, 'row', 0, 2, tiled=True)[0]  14.4 us
    all_to_all x1, starting transfers between devices, on_device(): cols_all = jnp.concatenate(lax.all_to_all(sent, 'rep', 0, 0), axis=1)  9.07 us
    all_to_all x1, waiting for transfers between devices, on_device(): incoming = lax.all_to_all(outgoing, 'rep', 0, 0, tiled=True)  8.81 us
    all_to_all x1, starting transfers between devices, on_device(): incoming = lax.all_to_all(outgoing, 'rep', 0, 0, tiled=True)  4.8 us
    dot_general x1, matrix products, on_device(): jnp.einsum('fgq,qgn->qfn', grouped, pick, preferred_element_type=jnp.floa...  3.74 us
  transfers between devices with their start and end apart: 3, of which 3 were waited for; matrix products, arithmetic and copies ran while one was open for 3% of the time, Pallas kernels for 0%

profile of v1, /device:TPU:8, one launch (start us, length us, event | category | flops | bytes accessed | tf_op | source)
XLA Modules:
  0.0 139.4 jit_solution(7016408110530962927)
XLA Ops:
  0.6 0.0 copy-start
  0.6 1.3 stack.2
  1.9 9.1 %all-to-all-start = ((s32[8,2,8]{2,1,0:T(2,128)}), s32[8,2,8]{2,1,0:T(2,128)S(1)}, u32[]{:S(2)}, u32[]{:S(2)}) async-start(s32[8,2,8]{2,1,0:T(2,128)} %stack.2), calls=%async_computation | async-start | bytes 16384 | tf_op jit(solution)/shard_map/all_to_all | solution.py:42
  11.0 0.7 fusion.18
  11.7 0.2 convert_reduce_fusion
  11.9 0.9 convolution_convert_fusion.1
  12.8 0.1 broadcast_in_dim.37
  12.9 0.3 broadcast_in_dim.38
  13.2 1.6 %reshape.168 = bf16[64,2,2176]{2,1,0:T(2,128)(2,1)} reshape(bf16[64,17,4,64]{3,2,1,0:T(4,128)(2,1)S(1)} %broadcast_in_dim.38) | data formatting | bytes 1114112
  14.8 0.1 all-to-all-done
  14.9 14.4 %all-to-all-start.1 = ((bf16[64,2,2176]{2,1,0:T(2,128)(2,1)}), bf16[64,2,2176]{2,1,0:T(2,128)(2,1)S(1)}, u32[]{:S(2)}, u32[]{:S(2)}) async-start(bf16[64,2,2176]{2,1,0:T(2,128)(2,1)} %reshape.168), calls=%async_computation.1 | async-start | bytes 1114112 | tf_op jit(solution)/shard_map/all_to_all | solution.py:38
  29.3 0.1 reshape.160
  29.4 0.1 eq.34
  29.5 0.1 select_reduce_fusion
  29.6 0.1 iota_add_fusion
  29.7 34.1 %all-to-all-done.1 = bf16[64,2,2176]{2,1,0:T(2,128)(2,1)S(1)} async-done(((bf16[64,2,2176]{2,1,0:T(2,128)(2,1)}), bf16[64,2,2176]{2,1,0:T(2,128)(2,1)S(1)}, u32[]{:S(2)}, u32[]{:S(2)}) %all-to-all-start.1) | async-done | bytes 557088 | tf_op jit(solution)/shard_map/all_to_all | solution.py:38
  63.8 0.7 reshape.169
  64.5 0.5 copy.29
  65.0 0.8 copy.32
  65.9 0.1 copy.30
  66.0 3.7 %fusion = bf16[64,17,128]{2,1,0:T(8,128)(2,1)S(1)} fusion(bf16[17,256,64]{1,0,2:T(8,128)(2,1)S(1)} %copy.32, s32[64,128]{1,0:T(8,128)S(1)} %iota_add_fusion, s32[64,256]{1,0:T(8,128)S(1)} %copy.30), kind=kOutput, calls=%fused_computation | convolution fusion | flops 73400320 | bytes 933888 | tf_op jit(solution)/shard_map/fgq,qgn->qfn/dot_general | solution.py:51
  69.8 0.3 convolution_convert_fusion
  70.1 0.0 copy-start.3
  70.1 0.0 copy-start.1
  70.1 0.9 copy.33
  71.0 4.8 %all-to-all-start.2 = ((bf16[8,2,8,16,128]{4,3,2,1,0:T(8,128)(2,1)}), bf16[8,2,8,16,128]{4,3,2,1,0:T(8,128)(2,1)S(1)}, u32[]{:S(2)}, u32[]{:S(2)}) async-start(bf16[8,2,8,16,128]{4,3,2,1,0:T(8,128)(2,1)} %copy.33), calls=%async_computation.2 | async-start | bytes 1048576 | tf_op jit(solution)/shard_map/all_to_all | solution.py:59
  75.8 0.0 copy-done.3
  75.8 0.1 broadcast_compare_fusion.4
  75.9 8.8 %all-to-all-done.2 = bf16[8,2,8,16,128]{4,3,2,1,0:T(8,128)(2,1)S(1)} async-done(((bf16[8,2,8,16,128]{4,3,2,1,0:T(8,128)(2,1)}), bf16[8,2,8,16,128]{4,3,2,1,0:T(8,128)(2,1)S(1)}, u32[]{:S(2)}, u32[]{:S(2)}) %all-to-all-start.2) | async-done | bytes 524320 | tf_op jit(solution)/shard_map/all_to_all | solution.py:59
  84.7 0.0 copy-done.1
  84.7 0.4 fusion.4
  85.1 0.1 copy.35
  85.2 0.1 copy.36
  85.3 0.0 copy-start.2
  85.3 0.0 copy-start.4
  85.3 0.1 broadcast_in_dim.41
  85.4 12.8 %all_to_all.40 = bf16[8,256,128]{2,1,0:T(8,128)(2,1)S(1)} all-to-all(bf16[8,256,128]{2,1,0:T(8,128)(2,1)S(1)} %broadcast_in_dim.41), channel_id=1, replica_groups=mesh['row'=64,'rep'=8] {'rep'}, dimensions={0} | all-to-all | bytes 1048576 | tf_op jit(solution)/shard_map/all_to_all | solution.py:17
  98.2 0.1 reduce_sum.40
  98.3 0.0 copy-done
  98.3 0.0 copy-done.2
  98.3 0.0 copy-done.4
  98.3 0.9 convert_reduce_fusion.1
  99.2 0.1 fusion.21
  99.4 20.2 %all_to_all.41 = f32[64,1,128]{2,1,0:T(1,128)S(1)} all-to-all(f32[64,1,128]{2,1,0:T(1,128)S(1)} %bitcast.56), channel_id=1, replica_groups=mesh['row'=64,'rep'=8] {'row'}, dimensions={0} | all-to-all | bytes 65536 | tf_op jit(solution)/shard_map/all_to_all | solution.py:10
  119.6 0.1 reduce_sum.42
  119.7 18.5 %all_to_all.42 = f32[64,1,128]{2,1,0:T(1,128)S(1)} all-to-all(f32[64,1,128]{2,1,0:T(1,128)S(1)} %broadcast_in_dim.43), channel_id=1, replica_groups=mesh['row'=64,'rep'=8] {'row'}, dimensions={0} | all-to-all | bytes 65536 | tf_op jit(solution)/shard_map/all_to_all | solution.py:17
  138.2 0.5 slice_bitcast_fusion
  138.7 0.6 slice.23
  (14 shorter events, 0.2 us)
Async XLA Ops:
  0.6 97.7 %copy-start = (bf16[128,32]{0,1:T(8,128)(2,1)S(1)}, bf16[128,32]{0,1:T(8,128)(2,1)}, u32[]{:S(2)}) copy-start(bf16[128,32]{0,1:T(8,128)(2,1)} %param.13) | copy-start | bytes 24580
  1.9 12.9 %all-to-all-start = ((s32[8,2,8]{2,1,0:T(2,128)}), s32[8,2,8]{2,1,0:T(2,128)S(1)}, u32[]{:S(2)}, u32[]{:S(2)}) async-start(s32[8,2,8]{2,1,0:T(2,128)} %stack.2), calls=%async_computation | async-start | bytes 16384 | tf_op jit(solution)/shard_map/all_to_all | solution.py:42
  14.9 48.9 %all-to-all-start.1 = ((bf16[64,2,2176]{2,1,0:T(2,128)(2,1)}), bf16[64,2,2176]{2,1,0:T(2,128)(2,1)S(1)}, u32[]{:S(2)}, u32[]{:S(2)}) async-start(bf16[64,2,2176]{2,1,0:T(2,128)(2,1)} %reshape.168), calls=%async_computation.1 | async-start | bytes 1114112 | tf_op jit(solution)/shard_map/all_to_all | solution.py:38
  70.1 5.7 %copy-start.3 = (s32[2]{0:T(128)S(1)}, s32[2]{0:T(128)}, u32[]{:S(2)}) copy-start(s32[2]{0:T(128)} %param.11) | copy-start | bytes 28
  70.1 14.6 %copy-start.1 = (bf16[2,8,128,128]{3,2,1,0:T(8,128)(2,1)S(1)}, bf16[2,8,128,128]{3,2,1,0:T(8,128)(2,1)}, u32[]{:S(2)}) copy-start(bf16[2,8,128,128]{3,2,1,0:T(8,128)(2,1)} %param.12) | copy-start | bytes 1572868
  71.0 13.7 %all-to-all-start.2 = ((bf16[8,2,8,16,128]{4,3,2,1,0:T(8,128)(2,1)}), bf16[8,2,8,16,128]{4,3,2,1,0:T(8,128)(2,1)S(1)}, u32[]{:S(2)}, u32[]{:S(2)}) async-start(bf16[8,2,8,16,128]{4,3,2,1,0:T(8,128)(2,1)} %copy.33), calls=%async_computation.2 | async-start | bytes 1048576 | tf_op jit(solution)/shard_map/all_to_all | solution.py:59
  85.3 13.0 %copy-start.2 = (bf16[256,32]{0,1:T(8,128)(2,1)S(1)}, bf16[256,32]{0,1:T(8,128)(2,1)}, u32[]{:S(2)}) copy-start(bf16[256,32]{0,1:T(8,128)(2,1)} %param.15) | copy-start | bytes 49156
  85.3 13.0 %copy-start.4 = (f32[32]{0:T(128)S(1)}, f32[32]{0:T(128)}, u32[]{:S(2)}) copy-start(f32[32]{0:T(128)} %param.14) | copy-start | bytes 388
